TPU v7x, 32 devices: a whole 2x2x4 slice. The times are simulated.
32 devices in a mesh: groups: 2 (over x), blk: 16 (over z, y, core).
Axes of the slice: x: 2, y: 2, z: 4, core: 2. Of those that a mesh axis runs over, the one named last changes fastest.
Arguments:
- layer_input_tokens: bfloat16 [384, 8192], P('groups', 'blk'), parts along dimension 0, may hold values from -6 to 6
- input_norm_gain: float32 [8192], replicated, may hold values from 0.5 to 1.5
- query_weight: bfloat16 [8192, 8192], P(None, 'blk'), may hold values from -0.0625 to 0.0625
- key_value_weight: bfloat16 [8192, 2048], P(None, 'blk'), may hold values from -0.0625 to 0.0625
- output_weight: bfloat16 [8192, 8192], P(None, 'blk'), may hold values from -0.5 to 0.5
- adapter_down_weight: bfloat16 [16, 64, 8192], P('blk'), may hold values from -0.0625 to 0.0625
- adapter_up_weight: bfloat16 [16, 64, 8192], P(None, None, 'blk'), may hold values from -0.75 to 0.75
- key_value_page_pool: bfloat16 [512, 128, 2048], P(('groups', 'blk')), parts along dimension 0, may hold values from -240 to 240
- request_adapter: int32 [128], P('groups'), parts along dimension 0, may hold values from 0 to 15
- adapter_storage_slot: int32 [16], replicated, may hold values from 0 to 15, each once
- cached_lengths: int32 [128], P('groups'), parts along dimension 0, may hold values from 1 to 512, as said below
- request_page_tables: int32 [128, 4], P('groups'), parts along dimension 0, may hold values from -1 to 255, as said below
Outputs:
- layer_out: bfloat16 [384, 8192], P('groups', 'blk'), parts along dimension 0
There are 2 independent parts, one for each index of `groups`. A program takes and returns all parts, laid end to end along the dimension named above; an argument that names none is the same for every part. Nothing has to cross between parts.
Inputs may be any that keep to these rules, and one draw needn't show every extreme that they name: `cached_lengths`: each request's cached length; the longest is exactly 512. `request_page_tables`: row r holds ceil(cached_lengths[r] / 128) page numbers first and -1 after them; no page is named twice in the whole table.
All inputs are finite; a program needn't handle non-finite values.
Results may differ from a plain program's by a relative error of at most 0.0085.
The roundings to bfloat16 on the way count: a program that leaves them out, or rounds other values in their place, can miss the bound.
Values may be sent and summed in bfloat16 or wider, within the bound.
No kernel may reach another device: no remote copies, remote signals or barrier semaphores. Data moves between devices by JAX's collectives and lax.ppermute only.
A program may use at most 128 MiB of HBM per device.

v0:
```python
import math
import jax
import jax.numpy as jnp
from jax import lax
from jax.sharding import PartitionSpec as P

QUERY_HEADS = 64
KEY_VALUE_HEADS = 8
HEAD_WIDTH = 128
PAGE_LENGTH = 128
NEW_TOKENS = 3
theta_base = 500000.0
neg_large = -1e30


def apply_rotation(values, token_positions, first_col, rot_limit):
    width_cols = values.shape[1]
    columns = first_col + jnp.arange(width_cols, dtype=jnp.int32)
    pair_index = (columns % HEAD_WIDTH // 2).astype(jnp.float32)
    inverse = jnp.exp(pair_index * (-2.0 * math.log(theta_base) / HEAD_WIDTH))
    angles = token_positions[:, None] * inverse[None, :]
    cos_val = jnp.cos(angles[:, 0::2])
    sine_val = jnp.sin(angles[:, 0::2])
    even_part = values[:, 0::2]
    odd_part = values[:, 1::2]
    turned = jnp.stack(
        [even_part * cos_val - odd_part * sine_val, even_part * sine_val + odd_part * cos_val],
        axis=-1,
    ).reshape(values.shape)
    return jnp.where((columns < rot_limit)[None, :], turned, values)


def normalize(layer_input_tokens, input_norm_gain):
    values = layer_input_tokens.astype(jnp.float32)
    mean_square = jnp.mean(values * values, axis=-1, keepdims=True)
    return (values * lax.rsqrt(mean_square + 1e-05) * input_norm_gain[None, :]).astype(jnp.bfloat16)


def positions_of(cached_lengths):
    steps_row = jnp.arange(NEW_TOKENS, dtype=jnp.int32)
    return (
        jnp.repeat(cached_lengths, NEW_TOKENS) + jnp.tile(steps_row, cached_lengths.shape[0])
    ).astype(jnp.float32)


def to_tokens(request_first_layout):
    request_count = request_first_layout.shape[0]
    trailing_shape = request_first_layout.shape[3:]
    query_group_width = QUERY_HEADS // KEY_VALUE_HEADS
    split_head_shape = request_first_layout.reshape(
        (request_count, KEY_VALUE_HEADS, NEW_TOKENS, query_group_width) + trailing_shape
    )
    order_axes = (0, 2, 1, 3) + tuple(range(4, 4 + len(trailing_shape)))
    return split_head_shape.transpose(order_axes).reshape(request_count * NEW_TOKENS, -1)


def butterfly(value, combine):
    size = lax.axis_size("blk")
    step = 1
    while step < size:
        pairs = [(i, i ^ step) for i in range(size)]
        value = combine(value, lax.ppermute(value, "blk", pairs))
        step *= 2
    return value


def local(
    layer_input_tokens,
    input_norm_gain,
    query_weight,
    key_value_weight,
    output_weight,
    adapter_down_weight,
    adapter_up_weight,
    key_value_page_pool,
    request_adapter,
    adapter_storage_slot,
    cached_lengths,
    request_page_tables,
):
    own_index = lax.axis_index("blk")
    gathered = lax.all_gather(layer_input_tokens, "blk", axis=1, tiled=True)
    normalized_input = normalize(gathered, input_norm_gain)
    request_count = cached_lengths.shape[0]
    adapter_total = adapter_storage_slot.shape[0]
    choose = request_adapter[:, None] == jnp.arange(adapter_total, dtype=jnp.int32)[None, :]
    req_slot = jnp.sum(jnp.where(choose, adapter_storage_slot[None, :], 0), axis=1)
    token_cache_slot = jnp.repeat(req_slot, NEW_TOKENS)
    local_token_count = adapter_down_weight.shape[0]
    local_pick = (
        token_cache_slot[:, None] - own_index * local_token_count
        == jnp.arange(local_token_count, dtype=jnp.int32)[None, :]
    )
    output_projected = jnp.einsum(
        "ly,mxy->lmx", normalized_input, adapter_down_weight, preferred_element_type=jnp.float32
    )
    partial_codes = jnp.sum(jnp.where(local_pick[:, :, None], output_projected, 0.0), axis=1)
    adapter_choice_index = butterfly(partial_codes.astype(jnp.bfloat16), jnp.add)
    up_weight_rows = adapter_up_weight[token_cache_slot]
    adapter_query_update = jnp.einsum(
        "gk,gkq->gq", adapter_choice_index, up_weight_rows, preferred_element_type=jnp.float32
    )
    token_positions = positions_of(cached_lengths)
    query_cols = query_weight.shape[1]
    keyval_cols = key_value_weight.shape[1]
    query_part = apply_rotation(
        jnp.dot(normalized_input, query_weight, preferred_element_type=jnp.float32)
        + adapter_query_update,
        token_positions,
        own_index * query_cols,
        QUERY_HEADS * HEAD_WIDTH,
    ).astype(jnp.bfloat16)
    keyval_part = apply_rotation(
        jnp.dot(normalized_input, key_value_weight, preferred_element_type=jnp.float32),
        token_positions,
        own_index * keyval_cols,
        KEY_VALUE_HEADS * HEAD_WIDTH,
    ).astype(jnp.bfloat16)
    joined = lax.all_gather(
        jnp.concatenate([query_part, keyval_part], axis=1), "blk", axis=1, tiled=False
    )
    query_vectors = joined[:, :, :query_cols].reshape(joined.shape[0], -1)
    key_value_rows = joined[:, :, query_cols:].reshape(joined.shape[0], -1)
    query_group_width = QUERY_HEADS // KEY_VALUE_HEADS
    query_feature_width = query_group_width * NEW_TOKENS
    score_scale = 1.0 / math.sqrt(HEAD_WIDTH)
    query_req = (
        query_vectors.reshape(
            request_count, NEW_TOKENS, KEY_VALUE_HEADS, query_group_width, HEAD_WIDTH
        )
        .transpose(0, 2, 1, 3, 4)
        .reshape(request_count, KEY_VALUE_HEADS, query_feature_width, HEAD_WIDTH)
    )
    fresh_token_rows = key_value_rows.reshape(
        request_count, NEW_TOKENS, 2, KEY_VALUE_HEADS, HEAD_WIDTH
    )
    request_page_count = key_value_page_pool.shape[0]
    table_width = request_page_tables.shape[1]
    page_ids = own_index * request_page_count + jnp.arange(request_page_count, dtype=jnp.int32)
    matches = request_page_tables[None, :, :] == page_ids[:, None, None]
    page_owner = jnp.any(matches, axis=2)
    page_live = jnp.any(page_owner, axis=1)
    page_req = jnp.sum(
        jnp.where(page_owner, jnp.arange(request_count, dtype=jnp.int32)[None, :], 0), axis=1
    )
    page_slot = jnp.sum(
        jnp.where(matches, jnp.arange(table_width, dtype=jnp.int32)[None, None, :], 0), axis=(1, 2)
    )
    page_len = jnp.sum(jnp.where(page_owner, cached_lengths[None, :], 0), axis=1)
    key_pos = page_slot[:, None] * PAGE_LENGTH + jnp.arange(PAGE_LENGTH, dtype=jnp.int32)[None, :]
    key_valid = page_live[:, None] & (key_pos < page_len[:, None])
    valid_full = key_valid[:, None, None, :]
    gathered_cache_pages = key_value_page_pool.reshape(
        request_page_count, PAGE_LENGTH, 2, KEY_VALUE_HEADS, HEAD_WIDTH
    )
    query_page = query_req[page_req]
    scores = (
        jnp.einsum(
            "skqd,spkd->skqp",
            query_page,
            gathered_cache_pages[:, :, 0],
            preferred_element_type=jnp.float32,
        )
        * score_scale
    )
    masked = jnp.where(valid_full, scores, neg_large)
    page_peak = jnp.max(masked, axis=-1)
    req_peak = jnp.max(
        jnp.where(page_owner[:, :, None, None], page_peak[:, None], neg_large), axis=0
    )
    fresh_scores = (
        jnp.einsum(
            "rkqd,rjkd->rkqj",
            query_req,
            fresh_token_rows[:, :, 0],
            preferred_element_type=jnp.float32,
        )
        * score_scale
    )
    step_of = jnp.arange(query_feature_width, dtype=jnp.int32) // query_group_width
    fresh_ok = (jnp.arange(NEW_TOKENS, dtype=jnp.int32)[None, :] <= step_of[:, None])[None, None]
    fresh_masked = jnp.where(fresh_ok, fresh_scores, neg_large)
    top_score = butterfly(jnp.maximum(req_peak, jnp.max(fresh_masked, axis=-1)), jnp.maximum)
    weights = jnp.where(valid_full, jnp.exp(masked - top_score[page_req][..., None]), 0.0)
    page_num = jnp.einsum(
        "skqp,spkd->skqd",
        weights.astype(jnp.bfloat16),
        gathered_cache_pages[:, :, 1],
        preferred_element_type=jnp.float32,
    )
    device_count = lax.axis_size("blk")
    head_count = QUERY_HEADS
    owner_cols = query_cols
    owner_heads = max(1, owner_cols // HEAD_WIDTH)
    head_repeat = min(owner_cols, HEAD_WIDTH)
    owner_first_head = [o * owner_cols // HEAD_WIDTH for o in range(device_count)]
    head_pick = jnp.asarray(
        [[first + j for j in range(owner_heads)] for first in owner_first_head], jnp.int32
    )
    slot_num = to_tokens(page_num).reshape(request_page_count, NEW_TOKENS, device_count, owner_cols)
    slot_den = to_tokens(jnp.sum(weights, axis=-1)[..., None]).reshape(
        request_page_count, NEW_TOKENS, head_count
    )
    slot_den_owner = slot_den[:, :, head_pick]
    packed = jnp.concatenate([slot_num, slot_den_owner], axis=3).transpose(2, 0, 1, 3)
    received = lax.all_to_all(packed, "blk", 0, 0, tiled=True)
    group_pages = device_count * request_page_count
    all_page_ids = jnp.arange(group_pages, dtype=jnp.int32)
    all_owner = jnp.any(request_page_tables[None, :, :] == all_page_ids[:, None, None], axis=2)
    pick_req = all_owner.T.astype(jnp.float32)
    summed = jnp.einsum(
        "rp,px->rx", pick_req, received.reshape(group_pages, -1), precision=lax.Precision.HIGHEST
    ).reshape(request_count, NEW_TOKENS, owner_cols + owner_heads)
    fresh_weights = jnp.where(fresh_ok, jnp.exp(fresh_masked - top_score[..., None]), 0.0)
    fresh_num = jnp.einsum(
        "rkqj,rjkd->rkqd",
        fresh_weights.astype(jnp.bfloat16),
        fresh_token_rows[:, :, 1],
        preferred_element_type=jnp.float32,
    )
    fresh_den = jnp.sum(fresh_weights, axis=-1)
    fresh_num_own = lax.dynamic_slice_in_dim(
        to_tokens(fresh_num), own_index * owner_cols, owner_cols, axis=1
    )
    fresh_den_own = lax.dynamic_slice_in_dim(
        to_tokens(fresh_den[..., None]), own_index * owner_cols // HEAD_WIDTH, owner_heads, axis=1
    )
    num_own = summed[:, :, :owner_cols].reshape(request_count * NEW_TOKENS, owner_cols)
    den_own = summed[:, :, owner_cols:].reshape(request_count * NEW_TOKENS, owner_heads)
    totals = den_own + fresh_den_own
    attended_own = ((num_own + fresh_num_own) / jnp.repeat(totals, head_repeat, axis=1)).astype(
        jnp.bfloat16
    )
    attended = lax.all_gather(attended_own, "blk", axis=1, tiled=True)
    return jnp.dot(attended, output_weight, preferred_element_type=jnp.float32).astype(jnp.bfloat16)


def solution(mesh):
    placed = (
        P("groups", "blk"),
        P(),
        P(None, "blk"),
        P(None, "blk"),
        P(None, "blk"),
        P("blk", None, None),
        P(None, None, "blk"),
        P(("groups", "blk"), None, None),
        P("groups"),
        P(),
        P("groups"),
        P("groups", None),
    )
    return jax.shard_map(
        local, mesh=mesh, in_specs=placed, out_specs=P("groups", "blk"), check_vma=False
    )
```

profile of v0, /device:TPU:0, one launch (start us, length us, event | category | flops | bytes accessed | tf_op | source)
XLA Modules:
  0.0 356.7 jit_solution(8480461503229381404)
XLA Ops:
  12.0 7.3 %slice.45 = f32[192,256]{1,0:T(8,128)} slice(f32[192,512]{1,0:T(8,128)S(1)} %broadcast_multiply_fusion), slice={[0:192:1], [0:512:2]} | slice | bytes 393216 | tf_op jit(solution)/shard_map/slice | solution.py:22
  19.3 8.3 %gather_fusion = bf16[192,64,512]{2,1,0:T(8,128)(2,1)} fusion(bf16[16,64,512]{2,1,0:T(8,128)(2,1)S(1)} %copy-done.2, s32[1024]{0:T(1024)S(1)} %pad_clamp_fusion.2), kind=kCustom, calls=%fused_computation | custom fusion | bytes 25166592 | tf_op jit(solution)/shard_map/gather | solution.py:99
  28.7 30.7 %all-gather.5.cloned.1.call-done = bf16[192,8192]{1,0:T(8,128)(2,1)} async-done(((bf16[192,512]{1,0:T(8,128)(2,1)}), bf16[192,8192]{1,0:T(8,128)(2,1)}) %all-gather.5.cloned.1.call-update) | async-done | bytes 3145744 | tf_op jit(solution)/shard_map/all_gather | solution.py:82
  59.5 2.8 fusion
  71.0 2.6 collective-permute-done.1
  74.2 3.5 collective-permute-done.2
  79.2 3.3 collective-permute-done.3
  82.7 6.5 %fusion.48 = f32[192,1,512]{2,1,0:T(1,128)S(1)} fusion(bf16[192,64,1]{1,2,0:T(2,128)(2,1)S(1)} %copy.154, bf16[192,64,512]{2,1,0:T(8,128)(2,1)} %gather_fusion), kind=kOutput, calls=%fused_computation.123 | convolution fusion | flops 12582912 | bytes 13000704 | tf_op jit(solution)/shard_map/gk,gkq->gq/dot_general | solution.py:100
  89.1 5.3 %convolution_add_fusion = f32[192,512]{1,0:T(8,128)S(1)} fusion(bf16[8192,512]{1,0:T(8,128)(2,1)} %param.15, f32[192,1,512]{2,1,0:T(1,128)S(1)} %fusion.48, bf16[192,8192]{1,0:T(8,128)(2,1)S(1)} %copy-done.4, f32[8192]{0:T(1024)S(1)} %copy-done.9, f32[192]{0:T(256)S(1)} %add_rsqrt_fusion), kind=kOutput, calls=%fused_computation.26 | convolution fusion | flops 1617002496 | bytes 12354304 | tf_op jit(solution)/shard_map/dot_general | solution.py:107
  94.4 7.2 %slice.46 = f32[192,256]{1,0:T(8,128)S(1)} slice(f32[192,512]{1,0:T(8,128)S(1)} %convolution_add_fusion), slice={[0:192:1], [1:512:2]} | slice | bytes 393216 | tf_op jit(solution)/shard_map/slice | solution.py:25
  101.6 6.7 %slice.44 = f32[192,256]{1,0:T(8,128)S(1)} slice(f32[192,512]{1,0:T(8,128)S(1)} %convolution_add_fusion), slice={[0:192:1], [0:512:2]} | slice | bytes 393216 | tf_op jit(solution)/shard_map/slice | solution.py:24
  109.8 12.3 %copy.132 = bf16[16,128,2048]{1,2,0:T(8,128)(2,1)} copy(bf16[16,128,2048]{2,1,0:T(8,128)(2,1)} %param.20) | data formatting | bytes 16777216 | tf_op args[7]
  122.7 35.0 %all-gather.9.cloned.1.call-done = bf16[192,10240]{1,0:T(8,128)(2,1)} async-done(((bf16[192,640]{1,0:T(8,128)(2,1)}), bf16[192,10240]{1,0:T(8,128)(2,1)}) %all-gather.9.cloned.1.call-update) | async-done | bytes 3932176 | tf_op jit(solution)/shard_map/all_gather | solution.py:119
  157.7 2.9 copy.163
  163.8 6.1 %reshape_reshape.12 = bf16[64,3,8,8,128]{4,3,2,1,0:T(8,128)(2,1)} reshape(bf16[192,16,512]{2,1,0:T(8,128)(2,1)} %slice.66) | data formatting | bytes 6291456 | tf_op jit(solution)/shard_map/reshape;reshape | solution.py:128
  169.9 4.2 %copy.181 = bf16[64,3,8,8,128]{4,3,1,2,0:T(8,128)(2,1)} copy(bf16[64,3,8,8,128]{4,3,2,1,0:T(8,128)(2,1)} %reshape_reshape.12) | data formatting | bytes 6291456 | tf_op jit(solution)/shard_map/reshape;reshape | solution.py:128
  174.1 2.6 gather_fusion.1
  176.7 3.5 fusion.46
  182.8 3.7 %fusion.47 = (f32[64,8,24]{2,1,0:T(8,128)S(1)}, f32[64,8,24,3]{2,3,1,0:T(4,128)S(1)}) fusion(bf16[64,3,1,8,128]{4,3,2,1,0:T(8,128)(2,1)S(1)} %get-tuple-element.10, bf16[64,3,8,8,128]{4,3,2,1,0:T(8,128)(2,1)} %reshape_reshape.12, pred[24,3]{0,1:T(4,128)(4,1)S(1)} %iota_compare_fusion.2), kind=kOutput, calls=%fused_computation.122 | convolution fusion | flops 9535488 | bytes 3735624 | tf_op jit(solution)/shard_map/rkqd,rjkd->rkqj/dot_general | solution.py:172
  188.7 7.9 %collective-permute-done.5 = f32[64,8,24]{2,1,0:T(8,128)S(1)} collective-permute-done((f32[64,8,24]{2,1,0:T(8,128)S(1)}, f32[64,8,24]{2,1,0:T(8,128)S(1)}, u32[]{:S(2)}, u32[]{:S(2)}) %collective-permute-start.5) | collective-permute-done | bytes 49184 | tf_op jit(solution)/shard_map/ppermute | solution.py:62
  198.6 5.9 %collective-permute-done.6 = f32[64,8,24]{2,1,0:T(8,128)S(1)} collective-permute-done((f32[64,8,24]{2,1,0:T(8,128)S(1)}, f32[64,8,24]{2,1,0:T(8,128)S(1)}, u32[]{:S(2)}, u32[]{:S(2)}) %collective-permute-start.6) | collective-permute-done | bytes 49184 | tf_op jit(solution)/shard_map/ppermute | solution.py:62
  206.6 11.4 %collective-permute-done.7 = f32[64,8,24]{2,1,0:T(8,128)S(1)} collective-permute-done((f32[64,8,24]{2,1,0:T(8,128)S(1)}, f32[64,8,24]{2,1,0:T(8,128)S(1)}, u32[]{:S(2)}, u32[]{:S(2)}) %collective-permute-start.7) | collective-permute-done | bytes 49184 | tf_op jit(solution)/shard_map/ppermute | solution.py:62
  219.6 5.8 %fusion.5 = f32[16,8,3,8,128]{4,3,2,1,0:T(8,128)} fusion(bf16[16,128,2,8,128]{1,4,3,2,0:T(8,128)(2,1)} %bitcast.110, f32[16,8,24,128]{3,2,1,0:T(8,128)S(1)} %get-tuple-element.20, f32[16,8,24]{2,1,0:T(8,128)S(1)} %gather_fusion.2, pred[16,128]{1,0:T(8,128)(4,1)S(1)} %fusion.26), kind=kOutput, calls=%fused_computation.21 | convolution fusion | flops 101842944 | bytes 7354368 | tf_op jit(solution)/shard_map/skqp,spkd->skqd/dot_general | solution.py:185
  234.0 3.7 %all-to-all-start = ((f32[16,16,3,516]{3,1,2,0:T(8,128)}), f32[16,16,3,516]{3,1,2,0:T(8,128)S(1)}, u32[]{:S(2)}, u32[]{:S(2)}) async-start(f32[16,16,3,516]{3,1,2,0:T(8,128)} %copy.143), calls=%async_computation | async-start | bytes 3932160 | tf_op jit(solution)/shard_map/all_to_all | solution.py:206
  243.5 2.8 convolution_bitcast_fusion
  246.4 3.4 copy.180
  249.8 7.2 %reshape.298 = f32[192,8192]{1,0:T(8,128)} reshape(f32[64,3,8,8,128]{4,3,2,1,0:T(8,128)} %bitcast.111) | data formatting | bytes 12582912 | tf_op jit(solution)/shard_map/reshape | solution.py:54
  257.0 19.5 %all-to-all-done = f32[16,16,3,516]{3,1,2,0:T(8,128)S(1)} async-done(((f32[16,16,3,516]{3,1,2,0:T(8,128)}), f32[16,16,3,516]{3,1,2,0:T(8,128)S(1)}, u32[]{:S(2)}, u32[]{:S(2)}) %all-to-all-start) | async-done | bytes 1585184 | tf_op jit(solution)/shard_map/all_to_all | solution.py:206
  276.5 2.6 copy.144
  279.0 3.1 reshape.295
  289.7 53.3 %all-gather.7.cloned.1.call-done = bf16[192,8192]{1,0:T(8,128)(2,1)} async-done(((bf16[192,512]{1,0:T(8,128)(2,1)}), bf16[192,8192]{1,0:T(8,128)(2,1)}) %all-gather.7.cloned.1.call-update) | async-done | bytes 3145744 | tf_op jit(solution)/shard_map/all_gather | solution.py:234
  343.0 6.9 %convolution_convert_fusion = bf16[192,512]{1,0:T(8,128)(2,1)} fusion(bf16[192,8192]{1,0:T(8,128)(2,1)} %all-gather.7.cloned.1.call-done, bf16[8192,512]{1,0:T(8,128)(2,1)} %param.17), kind=kOutput, calls=%fused_computation.27 | convolution fusion | flops 1610711040 | bytes 11730944 | tf_op jit(solution)/shard_map/dot_general | solution.py:235
  (131 shorter events, 54.9 us)
Async XLA Ops:
  6.5 58.5 %copy-start = (bf16[8192,128]{1,0:T(8,128)(2,1)S(1)}, bf16[8192,128]{1,0:T(8,128)(2,1)}, u32[]{:S(2)}) copy-start(bf16[8192,128]{1,0:T(8,128)(2,1)} %param.16) | copy-start | bytes 6291460
  6.5 12.7 %copy-start.2 = (bf16[16,64,512]{2,1,0:T(8,128)(2,1)S(1)}, bf16[16,64,512]{2,1,0:T(8,128)(2,1)}, u32[]{:S(2)}) copy-start(bf16[16,64,512]{2,1,0:T(8,128)(2,1)} %param.19) | copy-start | bytes 3145732
  6.5 52.9 %all-gather.5.cloned.1.call-start = ((), (), s32[]{:S(2)}) async-start(), calls=%async_computation.1 | async-start | bytes 3342336 | tf_op jit(solution)/shard_map/all_gather | solution.py:82
  7.3 150.4 %all-gather.9.cloned.1.call-start = ((), (), s32[]{:S(2)}) async-start(), calls=%async_computation.3 | async-start | bytes 4177920 | tf_op jit(solution)/shard_map/all_gather | solution.py:119
  19.2 8.4 %copy-start.6 = (f32[192,64]{1,0:T(8,128)S(1)}, f32[192,64]{1,0:T(8,128)}, u32[]{:S(2)}) copy-start(f32[192,64]{1,0:T(8,128)} %slice.48) | copy-start | bytes 147460
  19.3 8.8 %copy-start.5 = (f32[192,256]{1,0:T(8,128)S(1)}, f32[192,256]{1,0:T(8,128)}, u32[]{:S(2)}) copy-start(f32[192,256]{1,0:T(8,128)} %slice.45) | copy-start | bytes 589828
  27.6 34.6 %copy-start.9 = (f32[8192]{0:T(1024)S(1)}, f32[8192]{0:T(1024)}, u32[]{:S(2)}) copy-start(f32[8192]{0:T(1024)} %param.14) | copy-start | bytes 98308
  59.5 2.8 copy-start.3
  64.7 4.9 %collective-permute-start = (bf16[192,64]{0,1:T(8,128)(2,1)S(1)}, bf16[192,64]{0,1:T(8,128)(2,1)S(1)}, u32[]{:S(2)}, u32[]{:S(2)}) collective-permute-start(bf16[192,64]{0,1:T(8,128)(2,1)S(1)} %fusion.9), channel_id=1, source_target_pairs={{0,1},{1,0},{2,3},{3,2},{4,5},{5,4},{6,7},{7,6},{8,9},{9,8},{10,11... | collective-permute-start | bytes 73736 | tf_op jit(solution)/shard_map/ppermute | solution.py:62
  69.6 4.0 %collective-permute-start.1 = (bf16[192,64]{0,1:T(8,128)(2,1)S(1)}, bf16[192,64]{0,1:T(8,128)(2,1)S(1)}, u32[]{:S(2)}, u32[]{:S(2)}) collective-permute-start(bf16[192,64]{0,1:T(8,128)(2,1)S(1)} %add.180), channel_id=1, source_target_pairs={{0,2},{1,3},{2,0},{3,1},{4,6},{5,7},{6,4},{7,5},{8,10},{9,11},{10,... | collective-permute-start | bytes 73736 | tf_op jit(solution)/shard_map/ppermute | solution.py:62
  73.6 4.0 %collective-permute-start.2 = (bf16[192,64]{0,1:T(8,128)(2,1)S(1)}, bf16[192,64]{0,1:T(8,128)(2,1)S(1)}, u32[]{:S(2)}, u32[]{:S(2)}) collective-permute-start(bf16[192,64]{0,1:T(8,128)(2,1)S(1)} %add.181), channel_id=1, source_target_pairs={{0,4},{1,5},{2,6},{3,7},{4,0},{5,1},{6,2},{7,3},{8,12},{9,13},{10,... | collective-permute-start | bytes 73736 | tf_op jit(solution)/shard_map/ppermute | solution.py:62
  77.6 4.9 %collective-permute-start.3 = (bf16[192,64]{0,1:T(8,128)(2,1)S(1)}, bf16[192,64]{0,1:T(8,128)(2,1)S(1)}, u32[]{:S(2)}, u32[]{:S(2)}) collective-permute-start(bf16[192,64]{0,1:T(8,128)(2,1)S(1)} %add.182), channel_id=1, source_target_pairs={{0,8},{1,9},{2,10},{3,11},{4,12},{5,13},{6,14},{7,15},{8,0},{9,1},... | collective-permute-start | bytes 73736 | tf_op jit(solution)/shard_map/ppermute | solution.py:62
  82.6 6.5 %copy-start.4 = (bf16[192,8192]{1,0:T(8,128)(2,1)S(1)}, bf16[192,8192]{1,0:T(8,128)(2,1)}, u32[]{:S(2)}) copy-start(bf16[192,8192]{1,0:T(8,128)(2,1)} %all-gather.5.cloned.1.call-done) | copy-start | bytes 9437188
  109.8 12.3 %copy-start.7 = (s32[64,4]{0,1:T(4,128)S(1)}, s32[64,4]{0,1:T(4,128)}, u32[]{:S(2)}) copy-start(s32[64,4]{0,1:T(4,128)} %param.24) | copy-start | bytes 3076
  109.8 12.5 %copy-start.8 = (s32[64]{0:T(128)S(1)}, s32[64]{0:T(128)}, u32[]{:S(2)}) copy-start(s32[64]{0:T(128)} %param.23) | copy-start | bytes 772
  186.5 1.6 collective-permute-start.4
  188.1 8.5 %collective-permute-start.5 = (f32[64,8,24]{2,1,0:T(8,128)S(1)}, f32[64,8,24]{2,1,0:T(8,128)S(1)}, u32[]{:S(2)}, u32[]{:S(2)}) collective-permute-start(f32[64,8,24]{2,1,0:T(8,128)S(1)} %max.16), channel_id=1, source_target_pairs={{0,2},{1,3},{2,0},{3,1},{4,6},{5,7},{6,4},{7,5},{8,10},{9,11},{10,... | collective-permute-start | bytes 147464 | tf_op jit(solution)/shard_map/ppermute | solution.py:62
  196.7 7.9 %collective-permute-start.6 = (f32[64,8,24]{2,1,0:T(8,128)S(1)}, f32[64,8,24]{2,1,0:T(8,128)S(1)}, u32[]{:S(2)}, u32[]{:S(2)}) collective-permute-start(f32[64,8,24]{2,1,0:T(8,128)S(1)} %max.17), channel_id=1, source_target_pairs={{0,4},{1,5},{2,6},{3,7},{4,0},{5,1},{6,2},{7,3},{8,12},{9,13},{10,... | collective-permute-start | bytes 147464 | tf_op jit(solution)/shard_map/ppermute | solution.py:62
  204.6 13.5 %collective-permute-start.7 = (f32[64,8,24]{2,1,0:T(8,128)S(1)}, f32[64,8,24]{2,1,0:T(8,128)S(1)}, u32[]{:S(2)}, u32[]{:S(2)}) collective-permute-start(f32[64,8,24]{2,1,0:T(8,128)S(1)} %max.18), channel_id=1, source_target_pairs={{0,8},{1,9},{2,10},{3,11},{4,12},{5,13},{6,14},{7,15},{8,0},{9,1},... | collective-permute-start | bytes 147464 | tf_op jit(solution)/shard_map/ppermute | solution.py:62
  234.0 42.5 %all-to-all-start = ((f32[16,16,3,516]{3,1,2,0:T(8,128)}), f32[16,16,3,516]{3,1,2,0:T(8,128)S(1)}, u32[]{:S(2)}, u32[]{:S(2)}) async-start(f32[16,16,3,516]{3,1,2,0:T(8,128)} %copy.143), calls=%async_computation | async-start | bytes 3932160 | tf_op jit(solution)/shard_map/all_to_all | solution.py:206
  237.7 105.3 %all-gather.7.cloned.1.call-start = ((), (), s32[]{:S(2)}) async-start(), calls=%async_computation.2 | async-start | bytes 3342336 | tf_op jit(solution)/shard_map/all_gather | solution.py:234
  343.0 6.9 %copy-start.1 = (bf16[8192,128]{1,0:T(8,128)(2,1)S(1)}, bf16[8192,128]{1,0:T(8,128)(2,1)}, u32[]{:S(2)}) copy-start(bf16[8192,128]{1,0:T(8,128)(2,1)} %param.16) | copy-start | bytes 6291460
Sparse Core Ops, SparseCore 0:
  9.5 49.8 all-gather.4
  109.9 47.7 all-gather.8
  289.8 53.1 all-gather.6
where the time goes:
time: 362 us; the launch traced here: 357 us
  waiting for transfers between devices  175 us (48%)
  local copies, waits for them, and re-layouts  103 us (28%)
  matrix products  39.1 us (11%)
  between operations  13.9 us (4%)
  other arithmetic  12.9 us (4%)
  starting transfers between devices  12.4 us (3%)
    all_gather x1, waiting for transfers between devices, local(): attended = lax.all_gather(attended_own, 'blk', axis=1, tiled=True)  53.3 us
    ppermute x8, waiting for transfers between devices, butterfly(): value = combine(value, lax.ppermute(value, 'blk', pairs))  35.9 us
    all_gather x1, waiting for transfers between devices, local(): lax.all_gather(jnp.concatenate([query_part, keyval_part], axis=1), 'blk',...  35 us
    all_gather x1, waiting for transfers between devices, local(): gathered = lax.all_gather(layer_input_tokens, 'blk', axis=1, tiled=True)  30.7 us
    all_to_all x1, waiting for transfers between devices, local(): received = lax.all_to_all(packed, 'blk', 0, 0, tiled=True)  19.5 us
    unnamed x23, local copies, waits for them, and re-layouts  15.3 us
    another operation x2, local copies, waits for them, and re-layouts, local(): query_vectors.reshape(request_count, NEW_TOKENS, KEY_VALUE_HEADS, query_g...  10.3 us
    slice x2, local copies, waits for them, and re-layouts, apply_rotation(): cos_val = jnp.cos(angles[:, 0::2])  9.56 us
  transfers between devices with their start and end apart: 12, of which 11 were waited for; matrix products, arithmetic and copies ran while one was open for 16% of the time, Pallas kernels for 0%

commit v1 on v0

--- a/solution.py
+++ b/solution.py
@@ -11,6 +11,21 @@
 NEW_TOKENS = 3
 theta_base = 500000.0
 neg_large = -1e30
+
+
+def modes_return_all(frame_in, ax_name):
+    k_all = jax.lax.axis_size(ax_name)
+    pages = [frame_in]
+    for d in range(1, k_all):
+        pages.append(
+            jax.lax.ppermute(
+                pages[d - 1],
+                axis_name=ax_name,
+                perm=[(jj, (jj - 1) % k_all) for jj in range(k_all)],
+            )
+        )
+    kept_arr = jnp.concatenate(pages, axis=1)
+    return jnp.roll(kept_arr, shift=jax.lax.axis_index(ax_name) * frame_in.shape[1], axis=1)
 
 
 def apply_rotation(values, token_positions, first_col, rot_limit):
@@ -79,7 +94,7 @@
     request_page_tables,
 ):
     own_index = lax.axis_index("blk")
-    gathered = lax.all_gather(layer_input_tokens, "blk", axis=1, tiled=True)
+    gathered = modes_return_all(layer_input_tokens, "blk")
     normalized_input = normalize(gathered, input_norm_gain)
     request_count = cached_lengths.shape[0]
     adapter_total = adapter_storage_slot.shape[0]

time: 362 us -> 436 us (1.20)
  starting transfers between devices: 12.4 us -> 72.5 us
  local copies, waits for them, and re-layouts: 103 us -> 113 us
    ppermute x0 -> x15, starting transfers between devices: none -> 61.7 us  [modes_return_all(): jax.lax.ppermute(pages[d - 1], axis_name=ax_name, perm=[(jj, (jj - 1) % k...]
    ppermute x0 -> x15, waiting for transfers between devices: none -> 30.9 us  [modes_return_all(): jax.lax.ppermute(pages[d - 1], axis_name=ax_name, perm=[(jj, (jj - 1) % k...]
    all_gather x1 -> x0, waiting for transfers between devices: 30.7 us -> none  [local(): gathered = lax.all_gather(layer_input_tokens, 'blk', axis=1, tiled=True)]
    unnamed x23 -> x56, local copies, waits for them, and re-layouts: 15.3 us -> 23.7 us
  transfers between devices with their start and end apart: 12 -> 26, of which waited for: 11 -> 23; matrix products, arithmetic and copies ran while one was open for 16% -> 15% of each run, Pallas kernels for 0% -> 0%
where the time goes in v1:
time: 436 us; the launch traced here: 428 us
  waiting for transfers between devices  179 us (41%)
  local copies, waits for them, and re-layouts  113 us (26%)
  starting transfers between devices  72.5 us (17%)
  matrix products  38.4 us (9%)
  between operations  14.5 us (3%)
  other arithmetic  10.9 us (2%)
    ppermute x15, starting transfers between devices, modes_return_all(): jax.lax.ppermute(pages[d - 1], axis_name=ax_name, perm=[(jj, (jj - 1) % k...  61.7 us
    all_gather x1, waiting for transfers between devices, local(): attended = lax.all_gather(attended_own, 'blk', axis=1, tiled=True)  53.3 us
    all_gather x1, waiting for transfers between devices, local(): lax.all_gather(jnp.concatenate([query_part, keyval_part], axis=1), 'blk',...  37.6 us
    ppermute x8, waiting for transfers between devices, butterfly(): value = combine(value, lax.ppermute(value, 'blk', pairs))  37.4 us
    ppermute x15, waiting for transfers between devices, modes_return_all(): jax.lax.ppermute(pages[d - 1], axis_name=ax_name, perm=[(jj, (jj - 1) % k...  30.9 us
    unnamed x56, local copies, waits for them, and re-layouts  23.7 us
    all_to_all x1, waiting for transfers between devices, local(): received = lax.all_to_all(packed, 'blk', 0, 0, tiled=True)  19.5 us
    another operation x2, local copies, waits for them, and re-layouts, local(): query_vectors.reshape(request_count, NEW_TOKENS, KEY_VALUE_HEADS, query_g...  10.3 us
  transfers between devices with their start and end apart: 26, of which 23 were waited for; matrix products, arithmetic and copies ran while one was open for 15% of the time, Pallas kernels for 0%

profile of v1, /device:TPU:0, one launch (start us, length us, event | category | flops | bytes accessed | tf_op | source)
XLA Modules:
  0.0 428.1 jit_solution(4028183116907880000)
XLA Ops:
  6.5 5.4 %collective-permute-start = (bf16[192,512]{1,0:T(8,128)(2,1)}, bf16[192,512]{1,0:T(8,128)(2,1)S(1)}, u32[]{:S(2)}, u32[]{:S(2)}) collective-permute-start(bf16[192,512]{1,0:T(8,128)(2,1)} %param.13), channel_id=1, source_target_pairs={{0,15},{1,0},{2,1},{3,2},{4,3},{5,4},{6,5},{7,6},{8,7},{9,8},{10,9... | collective-permute-start | bytes 589832 | tf_op jit(solution)/shard_map/ppermute | solution.py:21
  15.5 4.5 %collective-permute-start.1 = (bf16[192,512]{1,0:T(8,128)(2,1)S(1)}, bf16[192,512]{1,0:T(8,128)(2,1)}, u32[]{:S(2)}, u32[]{:S(2)}) collective-permute-start(bf16[192,512]{1,0:T(8,128)(2,1)S(1)} %collective-permute-done), channel_id=1, source_target_pairs={{0,15},{1,0},{2,1},{3,2},{4,3},{5,4},{6,5},{7,6},{8,7},{9,8},{10,9... | collective-permute-start | bytes 589832 | tf_op jit(solution)/shard_map/ppermute | solution.py:21
  23.2 4.7 %collective-permute-start.2 = (bf16[192,512]{1,0:T(8,128)(2,1)}, bf16[192,512]{1,0:T(8,128)(2,1)}, u32[]{:S(2)}, u32[]{:S(2)}) collective-permute-start(bf16[192,512]{1,0:T(8,128)(2,1)} %collective-permute-done.1), channel_id=1, source_target_pairs={{0,15},{1,0},{2,1},{3,2},{4,3},{5,4},{6,5},{7,6},{8,7},{9,8},{10,9... | collective-permute-start | bytes 589832 | tf_op jit(solution)/shard_map/ppermute | solution.py:21
  28.0 7.3 %slice.45 = f32[192,256]{1,0:T(8,128)} slice(f32[192,512]{1,0:T(8,128)S(1)} %broadcast_multiply_fusion), slice={[0:192:1], [0:512:2]} | slice | bytes 393216 | tf_op jit(solution)/shard_map/slice | solution.py:37
  39.5 4.6 %collective-permute-start.4 = (bf16[192,512]{1,0:T(8,128)(2,1)}, bf16[192,512]{1,0:T(8,128)(2,1)}, u32[]{:S(2)}, u32[]{:S(2)}) collective-permute-start(bf16[192,512]{1,0:T(8,128)(2,1)} %collective-permute-done.3), channel_id=1, source_target_pairs={{0,15},{1,0},{2,1},{3,2},{4,3},{5,4},{6,5},{7,6},{8,7},{9,8},{10,9... | collective-permute-start | bytes 589832 | tf_op jit(solution)/shard_map/ppermute | solution.py:21
  44.1 8.1 %gather_fusion = bf16[192,64,512]{2,1,0:T(8,128)(2,1)} fusion(bf16[16,64,512]{2,1,0:T(8,128)(2,1)S(1)} %copy-done.2, s32[1024]{0:T(1024)S(1)} %pad_clamp_fusion.2), kind=kCustom, calls=%fused_computation | custom fusion | bytes 25166592 | tf_op jit(solution)/shard_map/gather | solution.py:114
  55.8 4.5 %collective-permute-start.6 = (bf16[192,512]{1,0:T(8,128)(2,1)S(1)}, bf16[192,512]{1,0:T(8,128)(2,1)S(1)}, u32[]{:S(2)}, u32[]{:S(2)}) collective-permute-start(bf16[192,512]{1,0:T(8,128)(2,1)S(1)} %collective-permute-done.5), channel_id=1, source_target_pairs={{0,15},{1,0},{2,1},{3,2},{4,3},{5,4},{6,5},{7,6},{8,7},{9,8},{10,9... | collective-permute-start | bytes 589832 | tf_op jit(solution)/shard_map/ppermute | solution.py:21
  63.5 4.6 %collective-permute-start.7 = (bf16[192,512]{1,0:T(8,128)(2,1)S(1)}, bf16[192,512]{1,0:T(8,128)(2,1)S(1)}, u32[]{:S(2)}, u32[]{:S(2)}) collective-permute-start(bf16[192,512]{1,0:T(8,128)(2,1)S(1)} %collective-permute-done.6), channel_id=1, source_target_pairs={{0,15},{1,0},{2,1},{3,2},{4,3},{5,4},{6,5},{7,6},{8,7},{9,8},{10,9... | collective-permute-start | bytes 589832 | tf_op jit(solution)/shard_map/ppermute | solution.py:21
  71.3 4.6 %collective-permute-start.8 = (bf16[192,512]{1,0:T(8,128)(2,1)S(1)}, bf16[192,512]{1,0:T(8,128)(2,1)S(1)}, u32[]{:S(2)}, u32[]{:S(2)}) collective-permute-start(bf16[192,512]{1,0:T(8,128)(2,1)S(1)} %collective-permute-done.7), channel_id=1, source_target_pairs={{0,15},{1,0},{2,1},{3,2},{4,3},{5,4},{6,5},{7,6},{8,7},{9,8},{10,9... | collective-permute-start | bytes 589832 | tf_op jit(solution)/shard_map/ppermute | solution.py:21
  79.1 4.6 %collective-permute-start.9 = (bf16[192,512]{1,0:T(8,128)(2,1)S(1)}, bf16[192,512]{1,0:T(8,128)(2,1)S(1)}, u32[]{:S(2)}, u32[]{:S(2)}) collective-permute-start(bf16[192,512]{1,0:T(8,128)(2,1)S(1)} %collective-permute-done.8), channel_id=1, source_target_pairs={{0,15},{1,0},{2,1},{3,2},{4,3},{5,4},{6,5},{7,6},{8,7},{9,8},{10,9... | collective-permute-start | bytes 589832 | tf_op jit(solution)/shard_map/ppermute | solution.py:21
  86.8 4.6 %collective-permute-start.10 = (bf16[192,512]{1,0:T(8,128)(2,1)S(1)}, bf16[192,512]{1,0:T(8,128)(2,1)S(1)}, u32[]{:S(2)}, u32[]{:S(2)}) collective-permute-start(bf16[192,512]{1,0:T(8,128)(2,1)S(1)} %collective-permute-done.9), channel_id=1, source_target_pairs={{0,15},{1,0},{2,1},{3,2},{4,3},{5,4},{6,5},{7,6},{8,7},{9,8},{10,9... | collective-permute-start | bytes 589832 | tf_op jit(solution)/shard_map/ppermute | solution.py:21
  94.6 4.6 %collective-permute-start.11 = (bf16[192,512]{1,0:T(8,128)(2,1)S(1)}, bf16[192,512]{1,0:T(8,128)(2,1)S(1)}, u32[]{:S(2)}, u32[]{:S(2)}) collective-permute-start(bf16[192,512]{1,0:T(8,128)(2,1)S(1)} %collective-permute-done.10), channel_id=1, source_target_pairs={{0,15},{1,0},{2,1},{3,2},{4,3},{5,4},{6,5},{7,6},{8,7},{9,8},{10,9... | collective-permute-start | bytes 589832 | tf_op jit(solution)/shard_map/ppermute | solution.py:21
  102.4 4.6 %collective-permute-start.12 = (bf16[192,512]{1,0:T(8,128)(2,1)S(1)}, bf16[192,512]{1,0:T(8,128)(2,1)S(1)}, u32[]{:S(2)}, u32[]{:S(2)}) collective-permute-start(bf16[192,512]{1,0:T(8,128)(2,1)S(1)} %collective-permute-done.11), channel_id=1, source_target_pairs={{0,15},{1,0},{2,1},{3,2},{4,3},{5,4},{6,5},{7,6},{8,7},{9,8},{10,9... | collective-permute-start | bytes 589832 | tf_op jit(solution)/shard_map/ppermute | solution.py:21
  110.2 4.6 %collective-permute-start.13 = (bf16[192,512]{1,0:T(8,128)(2,1)S(1)}, bf16[192,512]{1,0:T(8,128)(2,1)S(1)}, u32[]{:S(2)}, u32[]{:S(2)}) collective-permute-start(bf16[192,512]{1,0:T(8,128)(2,1)S(1)} %collective-permute-done.12), channel_id=1, source_target_pairs={{0,15},{1,0},{2,1},{3,2},{4,3},{5,4},{6,5},{7,6},{8,7},{9,8},{10,9... | collective-permute-start | bytes 589832 | tf_op jit(solution)/shard_map/ppermute | solution.py:21
  118.0 4.9 %collective-permute-start.14 = (bf16[192,512]{1,0:T(8,128)(2,1)S(1)}, bf16[192,512]{1,0:T(8,128)(2,1)S(1)}, u32[]{:S(2)}, u32[]{:S(2)}) collective-permute-start(bf16[192,512]{1,0:T(8,128)(2,1)S(1)} %collective-permute-done.13), channel_id=1, source_target_pairs={{0,15},{1,0},{2,1},{3,2},{4,3},{5,4},{6,5},{7,6},{8,7},{9,8},{10,9... | collective-permute-start | bytes 589832 | tf_op jit(solution)/shard_map/ppermute | solution.py:21
  137.5 3.9 collective-permute-done.16
  150.7 6.3 %fusion.48 = f32[192,1,512]{2,1,0:T(1,128)S(1)} fusion(bf16[192,64,1]{1,2,0:T(2,128)(2,1)S(1)} %copy.154, bf16[192,64,512]{2,1,0:T(8,128)(2,1)} %gather_fusion), kind=kOutput, calls=%fused_computation.155 | convolution fusion | flops 12582912 | bytes 13000704 | tf_op jit(solution)/shard_map/gk,gkq->gq/dot_general | solution.py:115
  157.0 6.2 %convolution_add_fusion = f32[192,512]{1,0:T(8,128)S(1)} fusion(bf16[8192,512]{1,0:T(8,128)(2,1)} %param.15, f32[192,1,512]{2,1,0:T(1,128)S(1)} %fusion.48, f32[8192]{0:T(1024)S(1)} %copy-done.10, f32[192]{0:T(256)S(1)} %add_rsqrt_fusion, bf16[192,16384]{1,0:T(8,128)(2,1)} %copy-done.3, s32[]{:T(128)S(6)} %select_n.145), kind=kOutput, calls=%fused_computation.26 | convolution fusion | flops 1617002496 | bytes 12354308 | tf_op jit(solution)/shard_map/dot_general | solution.py:122
  163.2 7.2 %slice.46 = f32[192,256]{1,0:T(8,128)S(1)} slice(f32[192,512]{1,0:T(8,128)S(1)} %convolution_add_fusion), slice={[0:192:1], [1:512:2]} | slice | bytes 393216 | tf_op jit(solution)/shard_map/slice | solution.py:40
  170.4 6.7 %slice.44 = f32[192,256]{1,0:T(8,128)S(1)} slice(f32[192,512]{1,0:T(8,128)S(1)} %convolution_add_fusion), slice={[0:192:1], [0:512:2]} | slice | bytes 393216 | tf_op jit(solution)/shard_map/slice | solution.py:39
  178.6 12.3 %copy.132 = bf16[16,128,2048]{1,2,0:T(8,128)(2,1)} copy(bf16[16,128,2048]{2,1,0:T(8,128)(2,1)} %param.20) | data formatting | bytes 16777216 | tf_op args[7]
  191.5 37.6 %all-gather.6.cloned.1.call-done = bf16[192,10240]{1,0:T(8,128)(2,1)} async-done(((bf16[192,640]{1,0:T(8,128)(2,1)}), bf16[192,10240]{1,0:T(8,128)(2,1)}) %all-gather.6.cloned.1.call-update) | async-done | bytes 3932176 | tf_op jit(solution)/shard_map/all_gather | solution.py:134
  235.2 6.1 %reshape_reshape.12 = bf16[64,3,8,8,128]{4,3,2,1,0:T(8,128)(2,1)} reshape(bf16[192,16,512]{2,1,0:T(8,128)(2,1)} %slice.66) | data formatting | bytes 6291456 | tf_op jit(solution)/shard_map/reshape;reshape | solution.py:143
  241.3 4.2 copy.181
  260.1 7.9 %collective-permute-done.20 = f32[64,8,24]{2,1,0:T(8,128)S(1)} collective-permute-done((f32[64,8,24]{2,1,0:T(8,128)S(1)}, f32[64,8,24]{2,1,0:T(8,128)S(1)}, u32[]{:S(2)}, u32[]{:S(2)}) %collective-permute-start.20) | collective-permute-done | bytes 49184 | tf_op jit(solution)/shard_map/ppermute | solution.py:77
  270.0 5.9 %collective-permute-done.21 = f32[64,8,24]{2,1,0:T(8,128)S(1)} collective-permute-done((f32[64,8,24]{2,1,0:T(8,128)S(1)}, f32[64,8,24]{2,1,0:T(8,128)S(1)}, u32[]{:S(2)}, u32[]{:S(2)}) %collective-permute-start.21) | collective-permute-done | bytes 49184 | tf_op jit(solution)/shard_map/ppermute | solution.py:77
  278.0 11.4 %collective-permute-done.22 = f32[64,8,24]{2,1,0:T(8,128)S(1)} collective-permute-done((f32[64,8,24]{2,1,0:T(8,128)S(1)}, f32[64,8,24]{2,1,0:T(8,128)S(1)}, u32[]{:S(2)}, u32[]{:S(2)}) %collective-permute-start.22) | collective-permute-done | bytes 49184 | tf_op jit(solution)/shard_map/ppermute | solution.py:77
  290.9 5.7 %fusion.5 = f32[16,8,3,8,128]{4,3,2,1,0:T(8,128)} fusion(bf16[16,128,2,8,128]{1,4,3,2,0:T(8,128)(2,1)} %bitcast.110, f32[16,8,24,128]{3,2,1,0:T(8,128)S(1)} %get-tuple-element.20, f32[16,8,24]{2,1,0:T(8,128)S(1)} %gather_fusion.2, pred[16,128]{1,0:T(8,128)(4,1)S(1)} %fusion.26), kind=kOutput, calls=%fused_computation.21 | convolution fusion | flops 101842944 | bytes 7354368 | tf_op jit(solution)/shard_map/skqp,spkd->skqd/dot_general | solution.py:200
  321.1 7.2 %reshape.298 = f32[192,8192]{1,0:T(8,128)} reshape(f32[64,3,8,8,128]{4,3,2,1,0:T(8,128)} %bitcast.111) | data formatting | bytes 12582912 | tf_op jit(solution)/shard_map/reshape | solution.py:69
  328.2 19.5 %all-to-all-done = f32[16,16,3,516]{3,1,2,0:T(8,128)S(1)} async-done(((f32[16,16,3,516]{3,1,2,0:T(8,128)}), f32[16,16,3,516]{3,1,2,0:T(8,128)S(1)}, u32[]{:S(2)}, u32[]{:S(2)}) %all-to-all-start) | async-done | bytes 1585184 | tf_op jit(solution)/shard_map/all_to_all | solution.py:221
  361.0 53.3 %all-gather.4.cloned.1.call-done = bf16[192,8192]{1,0:T(8,128)(2,1)} async-done(((bf16[192,512]{1,0:T(8,128)(2,1)}), bf16[192,8192]{1,0:T(8,128)(2,1)}) %all-gather.4.cloned.1.call-update) | async-done | bytes 3145744 | tf_op jit(solution)/shard_map/all_gather | solution.py:249
  414.3 6.8 %convolution_convert_fusion = bf16[192,512]{1,0:T(8,128)(2,1)} fusion(bf16[192,8192]{1,0:T(8,128)(2,1)} %all-gather.4.cloned.1.call-done, bf16[8192,512]{1,0:T(8,128)(2,1)} %param.17), kind=kOutput, calls=%fused_computation.27 | convolution fusion | flops 1610711040 | bytes 11730944 | tf_op jit(solution)/shard_map/dot_general | solution.py:250
  (192 shorter events, 129.4 us)
Async XLA Ops:
  6.5 126.3 %copy-start = (bf16[8192,128]{1,0:T(8,128)(2,1)S(1)}, bf16[8192,128]{1,0:T(8,128)(2,1)}, u32[]{:S(2)}) copy-start(bf16[8192,128]{1,0:T(8,128)(2,1)} %param.16) | copy-start | bytes 6291460
  6.5 37.6 %copy-start.2 = (bf16[16,64,512]{2,1,0:T(8,128)(2,1)S(1)}, bf16[16,64,512]{2,1,0:T(8,128)(2,1)}, u32[]{:S(2)}) copy-start(bf16[16,64,512]{2,1,0:T(8,128)(2,1)} %param.19) | copy-start | bytes 3145732
  6.5 222.6 %all-gather.6.cloned.1.call-start = ((), (), s32[]{:S(2)}) async-start(), calls=%async_computation.2 | async-start | bytes 4177920 | tf_op jit(solution)/shard_map/all_gather | solution.py:134
  6.5 8.9 %collective-permute-start = (bf16[192,512]{1,0:T(8,128)(2,1)}, bf16[192,512]{1,0:T(8,128)(2,1)S(1)}, u32[]{:S(2)}, u32[]{:S(2)}) collective-permute-start(bf16[192,512]{1,0:T(8,128)(2,1)} %param.13), channel_id=1, source_target_pairs={{0,15},{1,0},{2,1},{3,2},{4,3},{5,4},{6,5},{7,6},{8,7},{9,8},{10,9... | collective-permute-start | bytes 589832 | tf_op jit(solution)/shard_map/ppermute | solution.py:21
  15.5 7.7 %collective-permute-start.1 = (bf16[192,512]{1,0:T(8,128)(2,1)S(1)}, bf16[192,512]{1,0:T(8,128)(2,1)}, u32[]{:S(2)}, u32[]{:S(2)}) collective-permute-start(bf16[192,512]{1,0:T(8,128)(2,1)S(1)} %collective-permute-done), channel_id=1, source_target_pairs={{0,15},{1,0},{2,1},{3,2},{4,3},{5,4},{6,5},{7,6},{8,7},{9,8},{10,9... | collective-permute-start | bytes 589832 | tf_op jit(solution)/shard_map/ppermute | solution.py:21
  23.2 12.1 %collective-permute-start.2 = (bf16[192,512]{1,0:T(8,128)(2,1)}, bf16[192,512]{1,0:T(8,128)(2,1)}, u32[]{:S(2)}, u32[]{:S(2)}) collective-permute-start(bf16[192,512]{1,0:T(8,128)(2,1)} %collective-permute-done.1), channel_id=1, source_target_pairs={{0,15},{1,0},{2,1},{3,2},{4,3},{5,4},{6,5},{7,6},{8,7},{9,8},{10,9... | collective-permute-start | bytes 589832 | tf_op jit(solution)/shard_map/ppermute | solution.py:21
  35.3 4.3 collective-permute-start.3
  39.5 12.7 %collective-permute-start.4 = (bf16[192,512]{1,0:T(8,128)(2,1)}, bf16[192,512]{1,0:T(8,128)(2,1)}, u32[]{:S(2)}, u32[]{:S(2)}) collective-permute-start(bf16[192,512]{1,0:T(8,128)(2,1)} %collective-permute-done.3), channel_id=1, source_target_pairs={{0,15},{1,0},{2,1},{3,2},{4,3},{5,4},{6,5},{7,6},{8,7},{9,8},{10,9... | collective-permute-start | bytes 589832 | tf_op jit(solution)/shard_map/ppermute | solution.py:21
  44.1 31.7 %copy-start.6 = (bf16[192,512]{1,0:T(8,128)(2,1)S(1)}, bf16[192,512]{1,0:T(8,128)(2,1)}, u32[]{:S(2)}) copy-start(bf16[192,512]{1,0:T(8,128)(2,1)} %copy-done.5) | copy-start | bytes 589828
  52.2 3.6 collective-permute-start.5
  55.8 7.7 %collective-permute-start.6 = (bf16[192,512]{1,0:T(8,128)(2,1)S(1)}, bf16[192,512]{1,0:T(8,128)(2,1)S(1)}, u32[]{:S(2)}, u32[]{:S(2)}) collective-permute-start(bf16[192,512]{1,0:T(8,128)(2,1)S(1)} %collective-permute-done.5), channel_id=1, source_target_pairs={{0,15},{1,0},{2,1},{3,2},{4,3},{5,4},{6,5},{7,6},{8,7},{9,8},{10,9... | collective-permute-start | bytes 589832 | tf_op jit(solution)/shard_map/ppermute | solution.py:21
  63.5 7.8 %collective-permute-start.7 = (bf16[192,512]{1,0:T(8,128)(2,1)S(1)}, bf16[192,512]{1,0:T(8,128)(2,1)S(1)}, u32[]{:S(2)}, u32[]{:S(2)}) collective-permute-start(bf16[192,512]{1,0:T(8,128)(2,1)S(1)} %collective-permute-done.6), channel_id=1, source_target_pairs={{0,15},{1,0},{2,1},{3,2},{4,3},{5,4},{6,5},{7,6},{8,7},{9,8},{10,9... | collective-permute-start | bytes 589832 | tf_op jit(solution)/shard_map/ppermute | solution.py:21
  71.3 7.8 %collective-permute-start.8 = (bf16[192,512]{1,0:T(8,128)(2,1)S(1)}, bf16[192,512]{1,0:T(8,128)(2,1)S(1)}, u32[]{:S(2)}, u32[]{:S(2)}) collective-permute-start(bf16[192,512]{1,0:T(8,128)(2,1)S(1)} %collective-permute-done.7), channel_id=1, source_target_pairs={{0,15},{1,0},{2,1},{3,2},{4,3},{5,4},{6,5},{7,6},{8,7},{9,8},{10,9... | collective-permute-start | bytes 589832 | tf_op jit(solution)/shard_map/ppermute | solution.py:21
  79.1 7.8 %collective-permute-start.9 = (bf16[192,512]{1,0:T(8,128)(2,1)S(1)}, bf16[192,512]{1,0:T(8,128)(2,1)S(1)}, u32[]{:S(2)}, u32[]{:S(2)}) collective-permute-start(bf16[192,512]{1,0:T(8,128)(2,1)S(1)} %collective-permute-done.8), channel_id=1, source_target_pairs={{0,15},{1,0},{2,1},{3,2},{4,3},{5,4},{6,5},{7,6},{8,7},{9,8},{10,9... | collective-permute-start | bytes 589832 | tf_op jit(solution)/shard_map/ppermute | solution.py:21
  86.8 7.8 %collective-permute-start.10 = (bf16[192,512]{1,0:T(8,128)(2,1)S(1)}, bf16[192,512]{1,0:T(8,128)(2,1)S(1)}, u32[]{:S(2)}, u32[]{:S(2)}) collective-permute-start(bf16[192,512]{1,0:T(8,128)(2,1)S(1)} %collective-permute-done.9), channel_id=1, source_target_pairs={{0,15},{1,0},{2,1},{3,2},{4,3},{5,4},{6,5},{7,6},{8,7},{9,8},{10,9... | collective-permute-start | bytes 589832 | tf_op jit(solution)/shard_map/ppermute | solution.py:21
  94.6 7.8 %collective-permute-start.11 = (bf16[192,512]{1,0:T(8,128)(2,1)S(1)}, bf16[192,512]{1,0:T(8,128)(2,1)S(1)}, u32[]{:S(2)}, u32[]{:S(2)}) collective-permute-start(bf16[192,512]{1,0:T(8,128)(2,1)S(1)} %collective-permute-done.10), channel_id=1, source_target_pairs={{0,15},{1,0},{2,1},{3,2},{4,3},{5,4},{6,5},{7,6},{8,7},{9,8},{10,9... | collective-permute-start | bytes 589832 | tf_op jit(solution)/shard_map/ppermute | solution.py:21
  99.3 31.7 %copy-start.9 = (bf16[1,64,8192]{2,1,0:T(8,128)(2,1)S(1)}, bf16[1,64,8192]{2,1,0:T(8,128)(2,1)}, u32[]{:S(2)}) copy-start(bf16[1,64,8192]{2,1,0:T(8,128)(2,1)} %param.18) | copy-start | bytes 3145732
  99.3 31.7 %copy-start.10 = (f32[8192]{0:T(1024)S(1)}, f32[8192]{0:T(1024)}, u32[]{:S(2)}) copy-start(f32[8192]{0:T(1024)} %param.14) | copy-start | bytes 98308
  102.4 7.8 %collective-permute-start.12 = (bf16[192,512]{1,0:T(8,128)(2,1)S(1)}, bf16[192,512]{1,0:T(8,128)(2,1)S(1)}, u32[]{:S(2)}, u32[]{:S(2)}) collective-permute-start(bf16[192,512]{1,0:T(8,128)(2,1)S(1)} %collective-permute-done.11), channel_id=1, source_target_pairs={{0,15},{1,0},{2,1},{3,2},{4,3},{5,4},{6,5},{7,6},{8,7},{9,8},{10,9... | collective-permute-start | bytes 589832 | tf_op jit(solution)/shard_map/ppermute | solution.py:21
  110.2 7.8 %collective-permute-start.13 = (bf16[192,512]{1,0:T(8,128)(2,1)S(1)}, bf16[192,512]{1,0:T(8,128)(2,1)S(1)}, u32[]{:S(2)}, u32[]{:S(2)}) collective-permute-start(bf16[192,512]{1,0:T(8,128)(2,1)S(1)} %collective-permute-done.12), channel_id=1, source_target_pairs={{0,15},{1,0},{2,1},{3,2},{4,3},{5,4},{6,5},{7,6},{8,7},{9,8},{10,9... | collective-permute-start | bytes 589832 | tf_op jit(solution)/shard_map/ppermute | solution.py:21
  118.0 8.1 %collective-permute-start.14 = (bf16[192,512]{1,0:T(8,128)(2,1)S(1)}, bf16[192,512]{1,0:T(8,128)(2,1)S(1)}, u32[]{:S(2)}, u32[]{:S(2)}) collective-permute-start(bf16[192,512]{1,0:T(8,128)(2,1)S(1)} %collective-permute-done.13), channel_id=1, source_target_pairs={{0,15},{1,0},{2,1},{3,2},{4,3},{5,4},{6,5},{7,6},{8,7},{9,8},{10,9... | collective-permute-start | bytes 589832 | tf_op jit(solution)/shard_map/ppermute | solution.py:21
  132.2 5.1 %collective-permute-start.15 = (bf16[192,64]{0,1:T(8,128)(2,1)S(1)}, bf16[192,64]{0,1:T(8,128)(2,1)S(1)}, u32[]{:S(2)}, u32[]{:S(2)}) collective-permute-start(bf16[192,64]{0,1:T(8,128)(2,1)S(1)} %fusion.9), channel_id=1, source_target_pairs={{0,1},{1,0},{2,3},{3,2},{4,5},{5,4},{6,7},{7,6},{8,9},{9,8},{10,11... | collective-permute-start | bytes 73736 | tf_op jit(solution)/shard_map/ppermute | solution.py:77
  137.4 4.0 collective-permute-start.16
  141.4 4.0 collective-permute-start.17
  145.4 5.2 %collective-permute-start.18 = (bf16[192,64]{0,1:T(8,128)(2,1)S(1)}, bf16[192,64]{0,1:T(8,128)(2,1)S(1)}, u32[]{:S(2)}, u32[]{:S(2)}) collective-permute-start(bf16[192,64]{0,1:T(8,128)(2,1)S(1)} %add.194), channel_id=1, source_target_pairs={{0,8},{1,9},{2,10},{3,11},{4,12},{5,13},{6,14},{7,15},{8,0},{9,1},... | collective-permute-start | bytes 73736 | tf_op jit(solution)/shard_map/ppermute | solution.py:77
  257.8 1.6 collective-permute-start.19
  259.5 8.5 %collective-permute-start.20 = (f32[64,8,24]{2,1,0:T(8,128)S(1)}, f32[64,8,24]{2,1,0:T(8,128)S(1)}, u32[]{:S(2)}, u32[]{:S(2)}) collective-permute-start(f32[64,8,24]{2,1,0:T(8,128)S(1)} %max.16), channel_id=1, source_target_pairs={{0,2},{1,3},{2,0},{3,1},{4,6},{5,7},{6,4},{7,5},{8,10},{9,11},{10,... | collective-permute-start | bytes 147464 | tf_op jit(solution)/shard_map/ppermute | solution.py:77
  268.0 7.9 %collective-permute-start.21 = (f32[64,8,24]{2,1,0:T(8,128)S(1)}, f32[64,8,24]{2,1,0:T(8,128)S(1)}, u32[]{:S(2)}, u32[]{:S(2)}) collective-permute-start(f32[64,8,24]{2,1,0:T(8,128)S(1)} %max.17), channel_id=1, source_target_pairs={{0,4},{1,5},{2,6},{3,7},{4,0},{5,1},{6,2},{7,3},{8,12},{9,13},{10,... | collective-permute-start | bytes 147464 | tf_op jit(solution)/shard_map/ppermute | solution.py:77
  275.9 13.5 %collective-permute-start.22 = (f32[64,8,24]{2,1,0:T(8,128)S(1)}, f32[64,8,24]{2,1,0:T(8,128)S(1)}, u32[]{:S(2)}, u32[]{:S(2)}) collective-permute-start(f32[64,8,24]{2,1,0:T(8,128)S(1)} %max.18), channel_id=1, source_target_pairs={{0,8},{1,9},{2,10},{3,11},{4,12},{5,13},{6,14},{7,15},{8,0},{9,1},... | collective-permute-start | bytes 147464 | tf_op jit(solution)/shard_map/ppermute | solution.py:77
  305.3 42.5 %all-to-all-start = ((f32[16,16,3,516]{3,1,2,0:T(8,128)}), f32[16,16,3,516]{3,1,2,0:T(8,128)S(1)}, u32[]{:S(2)}, u32[]{:S(2)}) async-start(f32[16,16,3,516]{3,1,2,0:T(8,128)} %copy.143), calls=%async_computation | async-start | bytes 3932160 | tf_op jit(solution)/shard_map/all_to_all | solution.py:221
  309.0 105.3 %all-gather.4.cloned.1.call-start = ((), (), s32[]{:S(2)}) async-start(), calls=%async_computation.1 | async-start | bytes 3342336 | tf_op jit(solution)/shard_map/all_gather | solution.py:249
  360.9 60.1 %copy-start.1 = (bf16[8192,128]{1,0:T(8,128)(2,1)S(1)}, bf16[8192,128]{1,0:T(8,128)(2,1)}, u32[]{:S(2)}) copy-start(bf16[8192,128]{1,0:T(8,128)(2,1)} %param.16) | copy-start | bytes 6291460
  (5 other events, 43.3 us)
Sparse Core Ops, SparseCore 0:
  178.7 50.3 all-gather.5
  361.1 53.1 all-gather.3
